TPU v7x, 512 devices: a whole 4x8x8 slice. The times are simulated.
512 devices in a mesh: series: 8 (over y_hi, x), tm: 64 (over z, y_lo, core).
Axes of the slice: x: 4, y: 8 (y_hi: 2, y_lo: 4; y = y_hi * 4 + y_lo), z: 8, core: 2. Of those that a mesh axis runs over, the one named last changes fastest.
Arguments:
- y_obs: bfloat16 [32768, 32768], P('series', 'tm'), may hold values from -6 to 6
- tile_mask: int32 [256, 256], P('series', 'tm'), may hold values 0 or 1
- factors: float32 [32768, 128], P(('series', 'tm')), may hold values from -0.5 to 0.5
- adam_m: float32 [32768, 128], P(('series', 'tm')), may hold values from -3 to 3
- adam_v: float32 [32768, 128], P(('series', 'tm')), may hold values from 0.1 to 10
- basis: float32 [128, 32768], P('series', 'tm'), may hold values from -6 to 6
- dilations: int32 [4], replicated, may hold values from 1 to 32, as said below
- conv_w: bfloat16 [4, 2, 128, 128], replicated, may hold values from -0.375 to 0.375
- conv_b: float32 [4, 128], replicated, may hold values from -3 to 3
Outputs:
- factors_new: float32 [32768, 128], P(('series', 'tm'))
- m_new: float32 [32768, 128], P(('series', 'tm'))
- v_new: float32 [32768, 128], P(('series', 'tm'))
- basis_new: float32 [128, 32768], P('series', 'tm')
Inputs may be any that keep to these rules, and one draw needn't show every extreme that they name: `dilations`: at least one layer has dilation 32.
All inputs are finite; a program needn't handle non-finite values. No bound on the sum of `tile_mask` on one device may be relied on, other than what follows from the above.
Results may differ from a plain program's by a relative error of at most 0.0031.
Values may be sent and summed in bfloat16 or wider, within the bound.
No kernel may reach another device: no remote copies, remote signals or barrier semaphores. Data moves between devices by JAX's collectives and lax.ppermute only.
A program may use at most 64 MiB of HBM per device.

v0:
```python
import math
import jax
import jax.numpy as jnp
from jax import lax
from jax.sharding import PartitionSpec as P

K = 128
TILE = 128
LAYERS = 4
D_MAX = 32


def passed_along(value, axis, steps):
    count = lax.axis_size(axis)
    leading, last = (max(0, -steps), min(count, count - steps))
    return lax.ppermute(value, axis, [(source, source + steps) for source in range(leading, last)])


def expand(tiles, tile):
    rows, cols = tiles.shape
    ones = tiles.astype(jnp.float32)
    return jnp.broadcast_to(ones[:, None, :, None], (rows, tile, cols, tile)).reshape(
        rows * tile, cols * tile
    )


def adam_update(factors, adam_m, adam_v, grad_f):
    m_new = 0.9 * adam_m + 0.1 * grad_f
    v_new = 0.999 * adam_v + 0.001 * grad_f * grad_f
    m_hat = m_new / (1.0 - 0.9**10)
    v_hat = v_new / (1.0 - 0.999**10)
    return (factors - 0.01 * m_hat / (jnp.sqrt(v_hat) + 1e-08), m_new, v_new)


def conv_layer(hidden, hb, past, weights, biases):
    z_val = jnp.dot(weights[0], past, preferred_element_type=jnp.float32)
    z_val = z_val + jnp.dot(weights[1], hb, preferred_element_type=jnp.float32)
    z_val = z_val + biases[:, None]
    return hidden + jax.nn.relu(z_val)


def on_device(y_obs, tile_mask, factors, adam_m, adam_v, basis, dilations, conv_w, conv_b):
    own_rows = factors.shape[0]
    width = basis.shape[1]
    rank_part = basis.shape[0]
    total_time = width * lax.axis_size("tm")
    total_series = own_rows * lax.axis_size("tm") * lax.axis_size("series")
    f_block = lax.all_gather(factors.astype(jnp.bfloat16), "tm", axis=0, tiled=True)
    x_full = lax.all_gather(basis.astype(jnp.bfloat16), "series", axis=0, tiled=True)
    pred = jnp.dot(f_block, x_full, preferred_element_type=jnp.float32)
    resid = expand(tile_mask, TILE) * (y_obs.astype(jnp.float32) - pred)
    rb = resid.astype(jnp.bfloat16)
    scale_f = 1.0 / math.sqrt(total_time)
    contract_time = (((1,), (1,)), ((), ()))
    grad_f = lax.psum_scatter(
        -lax.dot_general(rb, x_full, contract_time, preferred_element_type=jnp.float32) * scale_f,
        "tm",
        scatter_dimension=0,
        tiled=True,
    )
    factors_new, m_new, v_new = adam_update(factors, adam_m, adam_v, grad_f)
    partial_x = -lax.dot_general(
        f_block, rb, (((0,), (0,)), ((), ())), preferred_element_type=jnp.float32
    )
    partial_x = partial_x * math.sqrt(K / total_series)
    grad_x = lax.psum_scatter(partial_x, "series", scatter_dimension=0, tiled=True)
    hidden = x_full.astype(jnp.float32)
    for layer in range(LAYERS):
        hb = hidden.astype(jnp.bfloat16)
        rim = passed_along(hb[:, width - D_MAX :], "tm", 1)
        extended = jnp.concatenate([rim, hb], axis=1)
        past = lax.dynamic_slice_in_dim(extended, D_MAX - dilations[layer], width, 1)
        hidden = conv_layer(hidden, hb, past, conv_w[layer], conv_b[layer])
    target = lax.dynamic_slice_in_dim(hidden, lax.axis_index("series") * rank_part, rank_part, 0)
    basis_new = basis - 0.5 * (grad_x + (basis - target))
    return (factors_new, m_new, v_new, basis_new)


def solution(mesh):
    return jax.shard_map(
        on_device,
        mesh=mesh,
        in_specs=(
            P("series", "tm"),
            P("series", "tm"),
            P(("series", "tm"), None),
            P(("series", "tm"), None),
            P(("series", "tm"), None),
            P("series", "tm"),
            P(),
            P(),
            P(),
        ),
        out_specs=(
            P(("series", "tm"), None),
            P(("series", "tm"), None),
            P(("series", "tm"), None),
            P("series", "tm"),
        ),
        check_vma=False,
    )
```

profile of v0, /device:TPU:6, one launch (start us, length us, event | category | flops | bytes accessed | tf_op | source)
XLA Modules:
  0.0 517.4 jit_solution(5125097129864647785)
XLA Ops:
  7.2 0.0 all-gather.2.cloned.1.call-start
  7.2 1.4 convert_element_type.30
  8.6 0.0 all-gather.2.cloned.1.call-update
  8.6 0.0 reduce-scatter.7.cloned.1.call-start
  8.7 0.7 convert_element_type.28
  9.3 0.1 copy.21
  9.4 0.8 convert_element_type.31
  10.2 43.9 %all_gather.7 = bf16[128,512]{1,0:T(8,128)(2,1)S(1)} all-gather(bf16[16,512]{1,0:T(8,128)(2,1)S(1)} %convert_element_type.31), channel_id=1, replica_groups=mesh['series'=8,'tm'=64] {'series'}, dimensions={0}, use_global_device_ids=true | all-gather | bytes 147456 | tf_op jit(solution)/shard_map/all_gather | solution.py:49
  54.1 76.9 %all-gather.2.cloned.1.call-done = bf16[4096,128]{1,0:T(8,128)(2,1)} async-done(((bf16[64,128]{1,0:T(8,128)(2,1)}), bf16[4096,128]{1,0:T(8,128)(2,1)}) %all-gather.2.cloned.1.call-update) | async-done | bytes 1048592 | tf_op jit(solution)/shard_map/all_gather | solution.py:48
  131.0 1.1 broadcast_in_dim.2
  132.2 1.0 copy-done.1
  133.2 0.3 copy-done.2
  133.5 1.2 fusion
  134.8 1.9 copy-done
  136.7 1.3 fusion.18
  138.0 0.8 copy.32
  138.8 0.0 reduce-scatter.7.cloned.1.call-update
  138.8 0.0 copy-start.9
  138.9 0.0 copy-start.3
  138.9 0.0 reduce-scatter.5.cloned.1.call-start
  138.9 4.8 fusion.1
  143.7 0.0 reduce-scatter.5.cloned.1.call-update
  143.8 0.0 copy-start.5
  143.8 0.1 slice.100
  143.9 2.1 collective-permute-start
  146.1 0.2 fusion.41
  146.3 0.6 fusion.61
  146.9 0.1 copy.27
  147.0 0.1 copy.22
  152.4 0.3 fusion.62
  152.7 3.1 collective-permute-start.1
  155.8 0.2 fusion.38
  156.0 0.6 collective-permute-done.1
  156.6 0.2 fusion.63
  156.8 2.2 collective-permute-start.2
  159.1 0.2 fusion.35
  159.3 0.6 collective-permute-done.2
  159.9 0.2 fusion.64
  160.1 4.0 collective-permute-start.3
  164.1 0.2 fusion.32
  164.3 0.6 collective-permute-done.3
  164.9 0.2 fusion.4
  165.1 60.5 %reduce-scatter.7.cloned.1.call-done = f32[16,512]{1,0:T(8,128)} async-done(((f32[128,512]{1,0:T(8,128)}), f32[16,512]{1,0:T(8,128)}) %reduce-scatter.7.cloned.1.call-update) | async-done | bytes 32784
  225.6 0.9 copy.33
  226.5 0.2 fusion.22
  226.7 0.7 copy.28
  227.4 282.0 %reduce-scatter.5.cloned.1.call-done = f32[64,128]{1,0:T(8,128)} async-done(((f32[4096,128]{1,0:T(8,128)}), f32[64,128]{1,0:T(8,128)}) %reduce-scatter.5.cloned.1.call-update) | async-done | bytes 32784 | tf_op jit(solution)/shard_map/reduce_scatter | solution.py:55
  509.4 1.4 divide_subtract_fusion
  (19 shorter events, 0.1 us)
Async XLA Ops:
  7.2 123.9 %all-gather.2.cloned.1.call-start = ((), (), s32[]{:S(2)}) async-start(), calls=%async_computation.2 | async-start | bytes 1064960 | tf_op jit(solution)/shard_map/all_gather | solution.py:48
  8.6 217.0 %reduce-scatter.7.cloned.1.call-start = ((), (), s32[]{:S(2)}) async-start(), calls=%async_computation.4 | async-start | bytes 294912
  131.0 2.2 copy-start.1
  131.0 2.5 copy-start.2
  134.8 1.9 copy-start
  138.8 7.2 %copy-start.9 = (f32[4,128]{1,0:T(4,128)S(1)}, f32[4,128]{1,0:T(4,128)}, u32[]{:S(2)}) copy-start(f32[4,128]{1,0:T(4,128)} %param.17) | copy-start | bytes 6148
  138.9 7.2 %copy-start.3 = (bf16[4,2,128,128]{3,2,1,0:T(8,128)(2,1)S(1)}, bf16[4,2,128,128]{3,2,1,0:T(8,128)(2,1)}, u32[]{:S(2)}) copy-start(bf16[4,2,128,128]{3,2,1,0:T(8,128)(2,1)} %param.16) | copy-start | bytes 786436
  138.9 7.4 %copy-start.8 = (s32[4]{0:T(128)S(1)}, s32[4]{0:T(128)}, u32[]{:S(2)}) copy-start(s32[4]{0:T(128)} %param.15) | copy-start | bytes 52
  138.9 8.0 %copy-start.4 = (f32[16,512]{1,0:T(8,128)S(1)}, f32[16,512]{1,0:T(8,128)}, u32[]{:S(2)}) copy-start(f32[16,512]{1,0:T(8,128)} %param.14) | copy-start | bytes 98308
  138.9 370.5 %reduce-scatter.5.cloned.1.call-start = ((), (), s32[]{:S(2)}) async-start(), calls=%async_computation.3 | async-start | bytes 2129920 | tf_op jit(solution)/shard_map/reduce_scatter | solution.py:55
  143.8 365.6 %copy-start.5 = (f32[64,128]{1,0:T(8,128)S(1)}, f32[64,128]{1,0:T(8,128)}, u32[]{:S(2)}) copy-start(f32[64,128]{1,0:T(8,128)} %param.11) | copy-start | bytes 98308
  143.8 365.6 %copy-start.6 = (f32[64,128]{1,0:T(8,128)S(1)}, f32[64,128]{1,0:T(8,128)}, u32[]{:S(2)}) copy-start(f32[64,128]{1,0:T(8,128)} %param.12) | copy-start | bytes 98308
  143.8 365.6 %copy-start.7 = (f32[64,128]{1,0:T(8,128)S(1)}, f32[64,128]{1,0:T(8,128)}, u32[]{:S(2)}) copy-start(f32[64,128]{1,0:T(8,128)} %param.13) | copy-start | bytes 98308
  143.9 8.5 %collective-permute-start = (bf16[128,32]{1,0:T(8,128)(2,1)S(1)}, bf16[128,32]{1,0:T(8,128)(2,1)S(1)}, u32[]{:S(2)}, u32[]{:S(2)}) collective-permute-start(bf16[128,32]{1,0:T(8,128)(2,1)S(1)} %slice.100), channel_id=1, source_target_pairs={{0,1},{1,2},{2,3},{3,4},{4,5},{5,6},{6,7},{7,8},{8,9},{9,10},{10,1... | collective-permute-start | bytes 24584 | tf_op jit(solution)/shard_map/ppermute | solution.py:16
  152.7 3.9 collective-permute-start.1
  156.8 3.1 collective-permute-start.2
  160.1 4.8 collective-permute-start.3
Sparse Core Ops, SparseCore 0:
  10.7 120.2 all-gather.1
  139.0 86.6 reduce-scatter.6
  228.6 280.7 reduce-scatter.4
where the time goes:
time: 518 us; the launch traced here: 517 us
  waiting for transfers between devices  421 us (81%)
  blocking collectives  43.9 us (8%)
  between operations  19.2 us (4%)
  starting transfers between devices  11.6 us (2%)
  matrix products  9.04 us (2%)
  local copies, waits for them, and re-layouts  7.91 us (2%)
    reduce_scatter x1, waiting for transfers between devices, on_device(): lax.psum_scatter(-lax.dot_general(rb, x_full, contract_time, preferred_el...  282 us
    all_gather x1, waiting for transfers between devices, on_device(): lax.all_gather(factors.astype(jnp.bfloat16), 'tm', axis=0, tiled=True)  76.9 us
    unnamed x4, waiting for transfers between devices  60.5 us
    all_gather x1, blocking collectives, on_device(): lax.all_gather(basis.astype(jnp.bfloat16), 'series', axis=0, tiled=True)  43.9 us
    ppermute x4, starting transfers between devices, passed_along(): lax.ppermute(value, axis, [(source, source + steps) for source in range(l...  11.4 us
  transfers between devices with their start and end apart: 7, of which 6 were waited for; matrix products, arithmetic and copies ran while one was open for 2% of the time, Pallas kernels for 0%

commit v1 on v0

--- a/solution.py
+++ b/solution.py
@@ -45,7 +45,11 @@
     rank_part = basis.shape[0]
     total_time = width * lax.axis_size("tm")
     total_series = own_rows * lax.axis_size("tm") * lax.axis_size("series")
-    f_block = lax.all_gather(factors.astype(jnp.bfloat16), "tm", axis=0, tiled=True)
+    part = factors.astype(jnp.bfloat16)
+    n_dev = lax.axis_size("tm")
+    parts = jnp.stack([part for _ in range(n_dev)])
+    parts = lax.all_to_all(parts, "tm", split_axis=0, concat_axis=0)
+    f_block = jnp.concatenate(parts, axis=0)
     x_full = lax.all_gather(basis.astype(jnp.bfloat16), "series", axis=0, tiled=True)
     pred = jnp.dot(f_block, x_full, preferred_element_type=jnp.float32)
     resid = expand(tile_mask, TILE) * (y_obs.astype(jnp.float32) - pred)

time: 518 us -> 465 us (0.90)
  waiting for transfers between devices: 421 us -> 348 us
  starting transfers between devices: 11.6 us -> 21.5 us
  blocking collectives: 43.9 us -> 53 us
    all_gather x1 -> x0, waiting for transfers between devices: 76.9 us -> none  [on_device(): lax.all_gather(factors.astype(jnp.bfloat16), 'tm', axis=0, tiled=True)]
    all_to_all x0 -> x1, starting transfers between devices: none -> 14.4 us  [on_device(): parts = lax.all_to_all(parts, 'tm', split_axis=0, concat_axis=0)]
    all_gather x1, blocking collectives: 43.9 us -> 53 us  [on_device(): lax.all_gather(basis.astype(jnp.bfloat16), 'series', axis=0, tiled=True)]
    unnamed x4 -> x3, waiting for transfers between devices: 60.5 us -> 64.6 us
  transfers between devices with their start and end apart: 7 -> 7, of which waited for: 6 -> 5; matrix products, arithmetic and copies ran while one was open for 2% -> 2% of each run, Pallas kernels for 0% -> 0%
where the time goes in v1:
time: 465 us; the launch traced here: 464 us
  waiting for transfers between devices  348 us (75%)
  blocking collectives  53 us (11%)
  starting transfers between devices  21.5 us (5%)
  between operations  19.5 us (4%)
  matrix products  9.08 us (2%)
  local copies, waits for them, and re-layouts  8.87 us (2%)
    reduce_scatter x1, waiting for transfers between devices, on_device(): lax.psum_scatter(-lax.dot_general(rb, x_full, contract_time, preferred_el...  282 us
    unnamed x3, waiting for transfers between devices  64.6 us
    all_gather x1, blocking collectives, on_device(): lax.all_gather(basis.astype(jnp.bfloat16), 'series', axis=0, tiled=True)  53 us
    all_to_all x1, starting transfers between devices, on_device(): parts = lax.all_to_all(parts, 'tm', split_axis=0, concat_axis=0)  14.4 us
  transfers between devices with their start and end apart: 7, of which 5 were waited for; matrix products, arithmetic and copies ran while one was open for 2% of the time, Pallas kernels for 0%

profile of v1, /device:TPU:6, one launch (start us, length us, event | category | flops | bytes accessed | tf_op | source)
XLA Modules:
  0.0 463.9 jit_solution(7413537225429268687)
XLA Ops:
  7.2 0.8 convert_element_type.30
  7.9 1.2 stack.2
  9.2 14.4 %all-to-all-start = ((bf16[64,64,128]{2,1,0:T(8,128)(2,1)}), bf16[64,64,128]{2,1,0:T(8,128)(2,1)S(1)}, u32[]{:S(2)}, u32[]{:S(2)}) async-start(bf16[64,64,128]{2,1,0:T(8,128)(2,1)} %stack.2), calls=%async_computation | async-start | bytes 2097152 | tf_op jit(solution)/shard_map/all_to_all | solution.py:51
  23.5 0.0 reduce-scatter.7.cloned.1.call-start
  23.6 0.7 convert_element_type.28
  24.3 0.1 copy.21
  24.4 0.8 convert_element_type.31
  25.1 53.0 %all_gather.3 = bf16[128,512]{1,0:T(8,128)(2,1)S(1)} all-gather(bf16[16,512]{1,0:T(8,128)(2,1)S(1)} %convert_element_type.31), channel_id=1, replica_groups=mesh['series'=8,'tm'=64] {'series'}, dimensions={0}, use_global_device_ids=true | all-gather | bytes 147456 | tf_op jit(solution)/shard_map/all_gather | solution.py:53
  78.1 1.1 broadcast_in_dim.2
  79.3 1.0 copy-done.1
  80.3 1.2 fusion
  81.6 1.9 copy-done
  83.5 1.3 fusion.18
  84.8 0.8 copy.32
  85.7 0.0 reduce-scatter.7.cloned.1.call-update
  85.7 0.0 copy-start.8
  85.7 0.0 copy-start.2
  85.7 0.0 copy-start.3
  85.8 0.0 reduce-scatter.5.cloned.1.call-start
  85.8 4.8 %fusion.1 = f32[4096,128]{1,0:T(8,128)} fusion(bf16[4096,512]{1,0:T(8,128)(2,1)} %copy-done, bf16[128,512]{1,0:T(8,128)(2,1)S(1)} %all_gather.3), kind=kOutput, calls=%fused_computation.3 | convolution fusion | flops 537919488 | bytes 6422528 | tf_op jit(solution)/shard_map/dot_general | solution.py:60
  90.6 0.0 reduce-scatter.5.cloned.1.call-update
  90.7 0.0 copy-start.4
  90.7 0.0 copy-start.5
  90.7 0.1 slice.100
  90.8 1.3 collective-permute-start
  92.1 0.2 fusion.41
  92.3 0.6 fusion.61
  92.9 0.1 copy.27
  93.1 0.1 copy.22
  98.4 0.3 fusion.62
  98.8 1.3 collective-permute-start.1
  100.1 0.2 fusion.38
  100.2 0.6 collective-permute-done.1
  100.9 0.2 fusion.63
  101.1 2.2 collective-permute-start.2
  103.3 0.2 fusion.35
  103.5 0.6 collective-permute-done.2
  104.2 0.2 fusion.64
  104.4 2.2 collective-permute-start.3
  106.6 0.2 fusion.32
  106.8 0.6 collective-permute-done.3
  107.4 0.2 fusion.4
  107.7 64.5 %reduce-scatter.7.cloned.1.call-done = f32[16,512]{1,0:T(8,128)} async-done(((f32[128,512]{1,0:T(8,128)}), f32[16,512]{1,0:T(8,128)}) %reduce-scatter.7.cloned.1.call-update) | async-done | bytes 32784
  172.2 0.9 copy.33
  173.1 0.2 fusion.22
  173.3 0.7 copy.28
  174.0 281.6 %reduce-scatter.5.cloned.1.call-done = f32[64,128]{1,0:T(8,128)} async-done(((f32[4096,128]{1,0:T(8,128)}), f32[64,128]{1,0:T(8,128)}) %reduce-scatter.5.cloned.1.call-update) | async-done | bytes 32784 | tf_op jit(solution)/shard_map/reduce_scatter | solution.py:59
  455.6 1.4 divide_subtract_fusion
  (17 shorter events, 0.0 us)
Async XLA Ops:
  9.2 69.0 %all-to-all-start = ((bf16[64,64,128]{2,1,0:T(8,128)(2,1)}), bf16[64,64,128]{2,1,0:T(8,128)(2,1)S(1)}, u32[]{:S(2)}, u32[]{:S(2)}) async-start(bf16[64,64,128]{2,1,0:T(8,128)(2,1)} %stack.2), calls=%async_computation | async-start | bytes 2097152 | tf_op jit(solution)/shard_map/all_to_all | solution.py:51
  23.5 148.6 %reduce-scatter.7.cloned.1.call-start = ((), (), s32[]{:S(2)}) async-start(), calls=%async_computation.4 | async-start | bytes 294912
  78.1 2.2 copy-start.1
  81.6 1.9 copy-start
  85.7 6.4 %copy-start.8 = (f32[4,128]{1,0:T(4,128)S(1)}, f32[4,128]{1,0:T(4,128)}, u32[]{:S(2)}) copy-start(f32[4,128]{1,0:T(4,128)} %param.17) | copy-start | bytes 6148
  85.7 6.4 %copy-start.2 = (bf16[4,2,128,128]{3,2,1,0:T(8,128)(2,1)S(1)}, bf16[4,2,128,128]{3,2,1,0:T(8,128)(2,1)}, u32[]{:S(2)}) copy-start(bf16[4,2,128,128]{3,2,1,0:T(8,128)(2,1)} %param.16) | copy-start | bytes 786436
  85.7 6.6 %copy-start.7 = (s32[4]{0:T(128)S(1)}, s32[4]{0:T(128)}, u32[]{:S(2)}) copy-start(s32[4]{0:T(128)} %param.15) | copy-start | bytes 52
  85.7 7.2 %copy-start.3 = (f32[16,512]{1,0:T(8,128)S(1)}, f32[16,512]{1,0:T(8,128)}, u32[]{:S(2)}) copy-start(f32[16,512]{1,0:T(8,128)} %param.14) | copy-start | bytes 98308
  85.8 369.8 %reduce-scatter.5.cloned.1.call-start = ((), (), s32[]{:S(2)}) async-start(), calls=%async_computation.3 | async-start | bytes 2129920 | tf_op jit(solution)/shard_map/reduce_scatter | solution.py:59
  90.7 365.0 %copy-start.4 = (f32[64,128]{1,0:T(8,128)S(1)}, f32[64,128]{1,0:T(8,128)}, u32[]{:S(2)}) copy-start(f32[64,128]{1,0:T(8,128)} %param.11) | copy-start | bytes 98308
  90.7 364.9 %copy-start.5 = (f32[64,128]{1,0:T(8,128)S(1)}, f32[64,128]{1,0:T(8,128)}, u32[]{:S(2)}) copy-start(f32[64,128]{1,0:T(8,128)} %param.12) | copy-start | bytes 98308
  90.7 364.9 %copy-start.6 = (f32[64,128]{1,0:T(8,128)S(1)}, f32[64,128]{1,0:T(8,128)}, u32[]{:S(2)}) copy-start(f32[64,128]{1,0:T(8,128)} %param.13) | copy-start | bytes 98308
  90.8 7.6 %collective-permute-start = (bf16[128,32]{1,0:T(8,128)(2,1)S(1)}, bf16[128,32]{1,0:T(8,128)(2,1)S(1)}, u32[]{:S(2)}, u32[]{:S(2)}) collective-permute-start(bf16[128,32]{1,0:T(8,128)(2,1)S(1)} %slice.100), channel_id=1, source_target_pairs={{0,1},{1,2},{2,3},{3,4},{4,5},{5,6},{6,7},{7,8},{8,9},{9,10},{10,1... | collective-permute-start | bytes 24584 | tf_op jit(solution)/shard_map/ppermute | solution.py:16
  98.8 2.1 collective-permute-start.1
  101.1 3.1 collective-permute-start.2
  104.4 3.1 collective-permute-start.3
Sparse Core Ops, SparseCore 0:
  85.8 86.3 reduce-scatter.6
  175.2 280.3 reduce-scatter.4
